TPU v7x, 128 devices: a whole 4x4x4 slice. The times are simulated.
128 devices in a mesh: seq: 16 (over z, x), exp: 8 (over y, core).
Axes of the slice: x: 4, y: 4, z: 4, core: 2. Of those that a mesh axis runs over, the one named last changes fastest.
Arguments:
- residual_in: bfloat16 [8, 4096, 2048], P('exp', 'seq'), may hold values from -6 to 6
- query_matrix: bfloat16 [8, 4096, 2048], P('exp', 'seq'), may hold values from -6 to 6
- key_vectors: bfloat16 [8, 4096, 2048], P('exp', 'seq'), may hold values from -6 to 6
- value_vectors: bfloat16 [8, 4096, 2048], P('exp', 'seq'), may hold values from -6 to 6
- head_gain: float32 [2048], replicated, may hold values from 0.5 to 1.5
- norm_gain: float32 [2048], replicated, may hold values from 0.5 to 1.5
- expert_ids: int32 [8, 4096, 4], P('exp', 'seq'), may hold values from 0 to 7, all different within a row; in each aligned block of 256 rows (0 to 255, 256 to 511, ..., all dimensions but the last counted through in order) at most 192 rows name the same one
- gate_probs: float32 [8, 4096, 4], P('exp', 'seq'), may hold values from 0.25 to 1
- w_gate: bfloat16 [8, 2048, 1408], P('exp'), may hold values from -0.125 to 0.125
- w_up: bfloat16 [8, 2048, 1408], P('exp'), may hold values from -0.125 to 0.125
- w_down: bfloat16 [8, 1408, 2048], P('exp'), may hold values from -0.15625 to 0.15625
Outputs:
- layer_out: bfloat16 [8, 4096, 2048], P('exp', 'seq')
Inputs may be any that keep to these rules, and one draw needn't show every extreme that they name: `expert_ids`: the 4 experts of one position differ; among the 256 positions of one device, no expert is named by more than 192 routes.
All inputs are finite; a program needn't handle non-finite values.
Results may differ from a plain program's by a relative error of at most 0.013.
Values may be sent and summed in bfloat16 or wider, within the bound.
No kernel may reach another device: no remote copies, remote signals or barrier semaphores. Data moves between devices by JAX's collectives and lax.ppermute only.
A program may use at most 128 MiB of HBM per device.

v0:
```python
import jax
import jax.numpy as jnp
from jax import lax
from jax.sharding import PartitionSpec as P

D = 2048
HEADS = 16
HD = 128
TOP = 4
EXPERTS = 8
CAP = 192


def on_device(
    residual_in,
    query_matrix,
    key_vectors,
    value_vectors,
    head_gain,
    norm_gain,
    expert_ids,
    gate_probs,
    w_gate,
    w_up,
    w_down,
):
    positions = residual_in.shape[1]
    queries = query_matrix[0].reshape(positions, HEADS, HD)
    key_rows = key_vectors[0].reshape(positions, HEADS, HD)
    value_rows = value_vectors[0].reshape(positions, HEADS, HD)
    state = jnp.einsum("thd,the->hde", key_rows, value_rows, preferred_element_type=jnp.float32)
    my_index = lax.axis_index("seq")
    piece = lax.all_gather(state[None], "seq", axis=0, tiled=True)
    owners = jnp.arange(piece.shape[0], dtype=jnp.int32)
    earlier = owners < my_index
    prefix = jnp.sum(jnp.where(earlier[:, None, None, None], piece, 0.0), axis=0)
    causal = jnp.tril(jnp.ones((positions, positions), dtype=bool))
    scores = jnp.einsum("thd,uhd->htu", queries, key_rows, preferred_element_type=jnp.float32)
    weights = jnp.where(causal[None], scores, 0.0).astype(jnp.bfloat16)
    inner = jnp.einsum("htu,uhd->thd", weights, value_rows, preferred_element_type=jnp.float32)
    outer_product = jnp.einsum(
        "thd,hde->the", queries, prefix.astype(jnp.bfloat16), preferred_element_type=jnp.float32
    )
    mixed = inner + outer_product
    mean_square = jnp.mean(mixed * mixed, axis=-1, keepdims=True)
    attn = (mixed * lax.rsqrt(mean_square + 1e-06)).reshape(positions, D) * head_gain
    resid_float = (
        (residual_in[0].astype(jnp.float32) + attn).astype(jnp.bfloat16).astype(jnp.float32)
    )
    row_square = jnp.mean(resid_float * resid_float, axis=-1, keepdims=True)
    normed = (resid_float * lax.rsqrt(row_square + 1e-06) * norm_gain).astype(jnp.bfloat16)
    route_ids = expert_ids[0].reshape(-1)
    route_gates = gate_probs[0]
    expert_indicator = (route_ids[:, None] == jnp.arange(EXPERTS, dtype=jnp.int32)[None, :]).astype(
        jnp.int32
    )
    slots = jnp.sum(
        (jnp.cumsum(expert_indicator, axis=0) - expert_indicator) * expert_indicator, axis=1
    )
    target = route_ids * CAP + slots
    token_of = jnp.arange(positions * TOP, dtype=jnp.int32) // TOP
    outgoing = (
        jnp.zeros((EXPERTS * CAP, D), jnp.bfloat16)
        .at[target]
        .set(normed[token_of])
        .reshape(EXPERTS, CAP, D)
    )
    local_count = w_gate.shape[0]
    groups = EXPERTS // local_count
    block = lax.all_to_all(outgoing, "exp", split_axis=0, concat_axis=0, tiled=True)
    count = block.shape[1]
    grouped = block.reshape(groups, local_count, count, D)
    gate_part = jnp.einsum("gend,edf->genf", grouped, w_gate, preferred_element_type=jnp.float32)
    up_part = jnp.einsum("gend,edf->genf", grouped, w_up, preferred_element_type=jnp.float32)
    hidden = (jax.nn.silu(gate_part) * up_part).astype(jnp.bfloat16)
    result = jnp.einsum("genf,efd->gend", hidden, w_down, preferred_element_type=jnp.float32)
    result = result.astype(jnp.bfloat16).reshape(EXPERTS, count, D)
    returned = lax.all_to_all(result, "exp", split_axis=0, concat_axis=0, tiled=True)
    picked = returned.reshape(EXPERTS * CAP, D)[target].reshape(positions, TOP, D)
    combined = jnp.sum(picked.astype(jnp.float32) * route_gates[:, :, None], axis=1)
    return (resid_float + combined).astype(jnp.bfloat16)[None]


def solution(mesh):
    in_specs = (
        P("exp", "seq", None),
        P("exp", "seq", None),
        P("exp", "seq", None),
        P("exp", "seq", None),
        P(),
        P(),
        P("exp", "seq", None),
        P("exp", "seq", None),
        P("exp", None, None),
        P("exp", None, None),
        P("exp", None, None),
    )
    out_specs = P("exp", "seq", None)
    return jax.shard_map(
        on_device, mesh=mesh, in_specs=in_specs, out_specs=out_specs, check_vma=False
    )
```

profile of v0, /device:TPU:1, one launch (start us, length us, event | category | flops | bytes accessed | tf_op | source)
XLA Modules:
  0.0 405.5 jit_solution(9483026792404834334)
XLA Ops:
  6.5 1.5 copy.43
  8.0 1.5 copy.45
  9.5 1.4 fusion.30
  11.0 0.1 copy.38
  11.1 0.1 eq.29
  11.4 1.5 copy.44
  12.8 2.3 reduce-window.6
  15.1 0.3 slice_reduce_fusion
  15.4 0.2 reduce-window.9
  15.5 0.1 copy.37
  15.7 0.1 mul.92
  16.0 2.7 fusion.28
  18.7 106.7 %all-gather.3.cloned.1.call-done = f32[256,128,128]{2,1,0:T(8,128)} async-done(((f32[16,128,128]{2,1,0:T(8,128)}), f32[256,128,128]{2,1,0:T(8,128)}) %all-gather.3.cloned.1.call-update) | async-done | bytes 16777232 | tf_op jit(solution)/shard_map/all_gather | solution.py:33
  125.5 8.9 %select_reduce_fusion = bf16[16,128,128]{2,1,0:T(8,128)(2,1)} fusion(f32[16,16,128,128]{3,2,1,0:T(8,128)} %bitcast.112, pred[16]{0:T(512)(128)(4,1)S(1)} %iota_compare_fusion.3), kind=kLoop, calls=%fused_computation.3 | loop fusion | flops 8126464 | bytes 17301520 | tf_op jit(solution)/shard_map/reduce_sum | solution.py:36
  134.4 1.6 multiply_reduce_fusion.1
  136.1 0.2 broadcast_multiply_fusion
  136.3 1.9 copy.40
  138.2 2.1 fusion.24
  140.3 1.3 fusion.26
  141.6 23.1 %scatter_custom_fusion = bf16[1536,2048]{1,0:T(8,128)(2,1)} fusion(s32[1024]{0:T(1024)S(1)} %bitcast.122, bf16[256,2048]{1,0:T(8,128)(2,1)} %fusion.26, s32[1024]{0:T(1024)S(1)} %broadcast_clamp_fusion.1, bf16[]{:T(256)} %constant.44.clone.1), kind=kCustom, calls=%fused_computation.20 | custom fusion | bytes 6291968 | tf_op jit(solution)/shard_map/scatter | solution.py:65
  164.8 76.4 %all_to_all.10 = bf16[8,192,2048]{2,1,0:T(8,128)(2,1)S(1)} all-to-all(bf16[8,192,2048]{2,1,0:T(8,128)(2,1)} %bitcast.109), channel_id=1, replica_groups=mesh['seq'=16,'exp'=8] {'exp'}, dimensions={0} | all-to-all | bytes 12582912 | tf_op jit(solution)/shard_map/all_to_all | solution.py:70
  241.2 2.6 copy-done.1
  243.7 13.4 %fusion.6 = f32[8,192,1408]{2,1,0:T(8,128)} fusion(bf16[8,192,2048]{2,1,0:T(8,128)(2,1)S(1)} %all_to_all.10, bf16[1,2048,1408]{2,1,0:T(8,128)(2,1)} %param.20), kind=kOutput, calls=%fused_computation.14 | convolution fusion | flops 8858370048 | bytes 20709376 | tf_op jit(solution)/shard_map/gend,edf->genf/dot_general | solution.py:74
  257.1 28.7 %fusion.9 = bf16[8,192,2048]{2,1,0:T(8,128)(2,1)} fusion(bf16[1,1408,2048]{2,1,0:T(8,128)(2,1)} %param.21, f32[8,192,1408]{2,1,0:T(8,128)} %fusion.6, bf16[8,192,2048]{2,1,0:T(8,128)(2,1)} %copy-done.1, bf16[1,2048,1408]{2,1,0:T(8,128)(2,1)} %param.19), kind=kOutput, calls=%fused_computation.17 | convolution fusion | flops 17732861952 | bytes 32768000 | tf_op jit(solution)/shard_map/genf,efd->gend/dot_general | solution.py:76
  285.8 6.0 %all-to-all-start.1 = ((bf16[8,192,2048]{2,1,0:T(8,128)(2,1)}), bf16[8,192,2048]{2,1,0:T(8,128)(2,1)}, u32[]{:S(2)}, u32[]{:S(2)}) async-start(bf16[8,192,2048]{2,1,0:T(8,128)(2,1)} %fusion.9), calls=%async_computation.1 | async-start | bytes 12582912 | tf_op jit(solution)/shard_map/all_to_all | solution.py:78
  291.9 0.1 copy.41
  292.0 1.8 copy.36
  293.8 69.2 %all-to-all-done.1 = bf16[8,192,2048]{2,1,0:T(8,128)(2,1)} async-done(((bf16[8,192,2048]{2,1,0:T(8,128)(2,1)}), bf16[8,192,2048]{2,1,0:T(8,128)(2,1)}, u32[]{:S(2)}, u32[]{:S(2)}) %all-to-all-start.1) | async-done | bytes 6291488 | tf_op jit(solution)/shard_map/all_to_all | solution.py:78
  363.1 12.4 %gather_fusion = bf16[1024,2048]{1,0:T(8,128)(2,1)} fusion(bf16[1536,2048]{1,0:T(8,128)(2,1)} %bitcast.26, s32[1024]{0:T(1024)S(1)} %broadcast_clamp_fusion), kind=kCustom, calls=%fused_computation.1 | custom fusion | bytes 8392704 | tf_op jit(solution)/shard_map/gather | solution.py:79
  375.5 8.3 %reshape.198 = f32[256,4,2048]{2,1,0:T(4,128)} reshape(bf16[1024,2048]{1,0:T(8,128)(2,1)} %gather_fusion) | data formatting | bytes 12582912 | tf_op jit(solution)/shard_map/convert_element_type | solution.py:80
  383.8 11.5 %multiply_reduce_fusion = f32[256,2048]{1,0:T(8,128)} fusion(f32[256,4,2048]{2,1,0:T(4,128)} %reshape.198, f32[256,4]{1,0:T(8,128)S(1)} %copy.41), kind=kLoop, calls=%fused_computation.11 | loop fusion | flops 3670016 | bytes 10489856 | tf_op jit(solution)/shard_map/reduce_sum | solution.py:80
  395.3 3.1 fusion.27
  (30 shorter events, 0.4 us)
Async XLA Ops:
  6.5 4.4 %copy-start.5 = (s32[1,256,4]{1,2,0:T(4,128)S(1)}, s32[1,256,4]{1,2,0:T(4,128)}, u32[]{:S(2)}) copy-start(s32[1,256,4]{1,2,0:T(4,128)} %param.17) | copy-start | bytes 12292
  6.5 119.0 %all-gather.3.cloned.1.call-start = ((), (), s32[]{:S(2)}) async-start(), calls=%async_computation.2 | async-start | bytes 17825792 | tf_op jit(solution)/shard_map/all_gather | solution.py:33
  125.5 9.0 %copy-start.3 = (f32[16,256,128]{1,2,0:T(8,128)S(1)}, f32[16,256,128]{1,2,0:T(8,128)}, u32[]{:S(2)}) copy-start(f32[16,256,128]{1,2,0:T(8,128)} %fusion.28) | copy-start | bytes 6291460
  136.1 2.1 copy-start.2
  136.1 2.1 copy-start.4
  136.3 4.0 copy-start.6
  241.2 2.6 copy-start.1
  285.8 6.0 %copy-start.7 = (f32[1,256,4]{1,2,0:T(4,128)S(1)}, f32[1,256,4]{1,2,0:T(4,128)}, u32[]{:S(2)}) copy-start(f32[1,256,4]{1,2,0:T(4,128)} %param.18) | copy-start | bytes 12292
  285.8 77.3 %all-to-all-start.1 = ((bf16[8,192,2048]{2,1,0:T(8,128)(2,1)}), bf16[8,192,2048]{2,1,0:T(8,128)(2,1)}, u32[]{:S(2)}, u32[]{:S(2)}) async-start(bf16[8,192,2048]{2,1,0:T(8,128)(2,1)} %fusion.9), calls=%async_computation.1 | async-start | bytes 12582912 | tf_op jit(solution)/shard_map/all_to_all | solution.py:78
  383.8 11.5 %copy-start = (f32[1,256,2048]{2,1,0:T(8,128)S(1)}, f32[1,256,2048]{2,1,0:T(8,128)}, u32[]{:S(2)}) copy-start(f32[1,256,2048]{2,1,0:T(8,128)} %copy.36) | copy-start | bytes 6291460
Sparse Core Ops, SparseCore 0:
  11.1 114.3 all-gather.2
where the time goes:
time: 412 us; the launch traced here: 405 us
  waiting for transfers between devices  176 us (43%)
  blocking collectives  76.4 us (19%)
  local copies, waits for them, and re-layouts  55.6 us (13%)
  matrix products  47.8 us (12%)
  other arithmetic  29.7 us (7%)
  between operations  13.8 us (3%)
  starting transfers between devices  6.04 us (1%)
    all_gather x1, waiting for transfers between devices, on_device(): piece = lax.all_gather(state[None], 'seq', axis=0, tiled=True)  107 us
    all_to_all x1, blocking collectives, on_device(): lax.all_to_all(outgoing, 'exp', split_axis=0, concat_axis=0, tiled=True)  76.4 us
    all_to_all x1, waiting for transfers between devices, on_device(): lax.all_to_all(result, 'exp', split_axis=0, concat_axis=0, tiled=True)  69.2 us
    dot_general x1, matrix products, on_device(): jnp.einsum('genf,efd->gend', hidden, w_down, preferred_element_type=jnp.f...  28.7 us
    scatter x1, local copies, waits for them, and re-layouts, on_device(): outgoing = jnp.zeros((EXPERTS * CAP, D), jnp.bfloat16).at[target].set(nor...  23.1 us
    dot_general x1, matrix products, on_device(): jnp.einsum('gend,edf->genf', grouped, w_up, preferred_element_type=jnp.fl...  13.4 us
    gather x1, local copies, waits for them, and re-layouts, on_device(): returned.reshape(EXPERTS * CAP, D)[target].reshape(positions, TOP, D)  12.4 us
    reduce_sum x1, other arithmetic, on_device(): jnp.sum(picked.astype(jnp.float32) * route_gates[:, :, None], axis=1)  11.5 us
  transfers between devices with their start and end apart: 2, of which 2 were waited for; matrix products, arithmetic and copies ran while one was open for 2% of the time, Pallas kernels for 0%

commit v1 on v0

--- a/solution.py
+++ b/solution.py
@@ -30,7 +30,25 @@
     value_rows = value_vectors[0].reshape(positions, HEADS, HD)
     state = jnp.einsum("thd,the->hde", key_rows, value_rows, preferred_element_type=jnp.float32)
     my_index = lax.axis_index("seq")
-    piece = lax.all_gather(state[None], "seq", axis=0, tiled=True)
+    size, position, rows = (lax.axis_size("seq"), lax.axis_index("seq"), state[None].shape[0])
+    right = [(i, (i + 1) % size) for i in range(size)]
+    left = [(i, (i - 1) % size) for i in range(size)]
+    piece = jnp.zeros(
+        (*state[None].shape[:0], size * rows, *state[None].shape[0 + 1 :]), state[None].dtype
+    )
+    piece = lax.dynamic_update_slice_in_dim(piece, state[None], position * rows, axis=0)
+    from_left = from_right = state[None]
+    half = size // 2
+    for step in range(1, half + 1):
+        from_left = lax.ppermute(from_left, "seq", right)
+        piece = lax.dynamic_update_slice_in_dim(
+            piece, from_left, (position - step) % size * rows, axis=0
+        )
+        if step < size - half:
+            from_right = lax.ppermute(from_right, "seq", left)
+            piece = lax.dynamic_update_slice_in_dim(
+                piece, from_right, (position + step) % size * rows, axis=0
+            )
     owners = jnp.arange(piece.shape[0], dtype=jnp.int32)
     earlier = owners < my_index
     prefix = jnp.sum(jnp.where(earlier[:, None, None, None], piece, 0.0), axis=0)

time: 412 us -> 502 us (1.22)
  starting transfers between devices: 6.04 us -> 41.8 us
  local copies, waits for them, and re-layouts: 55.6 us -> 91.1 us
  waiting for transfers between devices: 176 us -> 199 us
  between operations: 13.8 us -> 0.8 us
  blocking collectives: 76.4 us -> 82.9 us
    ppermute x0 -> x15, waiting for transfers between devices: none -> 130 us  [the longest x8 130 us: on_device(): from_left = lax.ppermute(from_left, 'seq', right)]
    all_gather x1 -> x0, waiting for transfers between devices: 107 us -> none  [on_device(): piece = lax.all_gather(state[None], 'seq', axis=0, tiled=True)]
    ppermute x0 -> x15, starting transfers between devices: none -> 35.8 us  [the longest x7 33.5 us: on_device(): from_right = lax.ppermute(from_right, 'seq', left)]
    dynamic_update_slice x0 -> x15, local copies, waits for them, and re-layouts: none -> 27.4 us  [the longest x8 15 us: on_device(): lax.dynamic_update_slice_in_dim(piece, from_left, (position - step) % siz...]
    broadcast_in_dim x0 -> x1, local copies, waits for them, and re-layouts: none -> 7.87 us  [on_device(): jnp.zeros((*state[None].shape[:0], size * rows, *state[None].shape[0 + 1:...]
    all_to_all x1, blocking collectives: 76.4 us -> 82.9 us  [on_device(): lax.all_to_all(outgoing, 'exp', split_axis=0, concat_axis=0, tiled=True)]
  transfers between devices with their start and end apart: 2 -> 16, of which waited for: 2 -> 9; matrix products, arithmetic and copies ran while one was open for 2% -> 7% of each run, Pallas kernels for 0% -> 0%
where the time goes in v1:
time: 502 us; the launch traced here: 493 us
  waiting for transfers between devices  199 us (40%)
  local copies, waits for them, and re-layouts  91.1 us (18%)
  blocking collectives  82.9 us (17%)
  matrix products  48.5 us (10%)
  starting transfers between devices  41.8 us (8%)
  other arithmetic  28.7 us (6%)
    ppermute x8, waiting for transfers between devices, on_device(): from_left = lax.ppermute(from_left, 'seq', right)  130 us
    all_to_all x1, blocking collectives, on_device(): lax.all_to_all(outgoing, 'exp', split_axis=0, concat_axis=0, tiled=True)  82.9 us
    all_to_all x1, waiting for transfers between devices, on_device(): lax.all_to_all(result, 'exp', split_axis=0, concat_axis=0, tiled=True)  69.2 us
    ppermute x7, starting transfers between devices, on_device(): from_right = lax.ppermute(from_right, 'seq', left)  33.5 us
    dot_general x1, matrix products, on_device(): jnp.einsum('genf,efd->gend', hidden, w_down, preferred_element_type=jnp.f...  28.7 us
    scatter x1, local copies, waits for them, and re-layouts, on_device(): outgoing = jnp.zeros((EXPERTS * CAP, D), jnp.bfloat16).at[target].set(nor...  23.3 us
    dynamic_update_slice x8, local copies, waits for them, and re-layouts, on_device(): lax.dynamic_update_slice_in_dim(piece, from_left, (position - step) % siz...  15 us
    dot_general x1, matrix products, on_device(): jnp.einsum('gend,edf->genf', grouped, w_up, preferred_element_type=jnp.fl...  13.4 us
  transfers between devices with their start and end apart: 16, of which 9 were waited for; matrix products, arithmetic and copies ran while one was open for 7% of the time, Pallas kernels for 0%

profile of v1, /device:TPU:1, one launch (start us, length us, event | category | flops | bytes accessed | tf_op | source)
XLA Modules:
  0.0 493.1 jit_solution(12730358671247627213)
XLA Ops:
  3.0 7.9 %broadcast_in_dim.33 = f32[16,16,128,128]{3,2,1,0:T(8,128)} broadcast(f32[]{:T(128)} %constant.121.clone.1), dimensions={} | broadcast | bytes 16777220 | tf_op jit(solution)/shard_map/broadcast_in_dim | solution.py:36
  14.3 4.7 collective-permute-start.1
  19.0 22.9 %collective-permute-done = f32[1,16,128,128]{3,2,1,0:T(8,128)S(1)} collective-permute-done((f32[1,16,128,128]{3,2,1,0:T(8,128)S(1)}, f32[1,16,128,128]{3,2,1,0:T(8,128)S(1)}, u32[]{:S(2)}, u32[]{:S(2)}) %collective-permute-start) | collective-permute-done | bytes 1048608 | tf_op jit(solution)/shard_map/ppermute | solution.py:43
  41.9 4.8 collective-permute-start.3
  46.7 22.0 %collective-permute-done.2 = f32[1,16,128,128]{3,2,1,0:T(8,128)S(1)} collective-permute-done((f32[1,16,128,128]{3,2,1,0:T(8,128)S(1)}, f32[1,16,128,128]{3,2,1,0:T(8,128)S(1)}, u32[]{:S(2)}, u32[]{:S(2)}) %collective-permute-start.2) | collective-permute-done | bytes 1048608 | tf_op jit(solution)/shard_map/ppermute | solution.py:43
  68.7 4.8 collective-permute-start.5
  73.5 21.1 %collective-permute-done.4 = f32[1,16,128,128]{3,2,1,0:T(8,128)S(1)} collective-permute-done((f32[1,16,128,128]{3,2,1,0:T(8,128)S(1)}, f32[1,16,128,128]{3,2,1,0:T(8,128)S(1)}, u32[]{:S(2)}, u32[]{:S(2)}) %collective-permute-start.4) | collective-permute-done | bytes 1048608 | tf_op jit(solution)/shard_map/ppermute | solution.py:43
  94.6 4.8 collective-permute-start.7
  99.4 20.4 %collective-permute-done.6 = f32[1,16,128,128]{3,2,1,0:T(8,128)} collective-permute-done((f32[1,16,128,128]{3,2,1,0:T(8,128)S(1)}, f32[1,16,128,128]{3,2,1,0:T(8,128)}, u32[]{:S(2)}, u32[]{:S(2)}) %collective-permute-start.6) | collective-permute-done | bytes 1048608 | tf_op jit(solution)/shard_map/ppermute | solution.py:43
  122.5 4.8 collective-permute-start.9
  129.6 14.8 %collective-permute-done.8 = f32[1,16,128,128]{3,2,1,0:T(8,128)} collective-permute-done((f32[1,16,128,128]{3,2,1,0:T(8,128)}, f32[1,16,128,128]{3,2,1,0:T(8,128)}, u32[]{:S(2)}, u32[]{:S(2)}) %collective-permute-start.8) | collective-permute-done | bytes 1048608 | tf_op jit(solution)/shard_map/ppermute | solution.py:43
  144.5 2.7 fusion.28
  147.2 4.8 collective-permute-start.11
  152.3 15.8 %collective-permute-done.10 = f32[1,16,128,128]{3,2,1,0:T(8,128)} collective-permute-done((f32[1,16,128,128]{3,2,1,0:T(8,128)}, f32[1,16,128,128]{3,2,1,0:T(8,128)}, u32[]{:S(2)}, u32[]{:S(2)}) %collective-permute-start.10) | collective-permute-done | bytes 1048608 | tf_op jit(solution)/shard_map/ppermute | solution.py:43
  177.2 4.9 collective-permute-start.13
  183.1 7.7 %collective-permute-done.12 = f32[1,16,128,128]{3,2,1,0:T(8,128)S(1)} collective-permute-done((f32[1,16,128,128]{3,2,1,0:T(8,128)}, f32[1,16,128,128]{3,2,1,0:T(8,128)S(1)}, u32[]{:S(2)}, u32[]{:S(2)}) %collective-permute-start.12) | collective-permute-done | bytes 1048608 | tf_op jit(solution)/shard_map/ppermute | solution.py:43
  191.0 2.4 constant_dynamic-update-slice_fusion.8
  195.6 2.3 constant_dynamic-update-slice_fusion.6
  198.0 2.3 constant_dynamic-update-slice_fusion.5
  207.1 5.5 %collective-permute-done.14 = f32[1,16,128,128]{3,2,1,0:T(8,128)S(1)} collective-permute-done((f32[1,16,128,128]{3,2,1,0:T(8,128)S(1)}, f32[1,16,128,128]{3,2,1,0:T(8,128)S(1)}, u32[]{:S(2)}, u32[]{:S(2)}) %collective-permute-start.14) | collective-permute-done | bytes 1048608 | tf_op jit(solution)/shard_map/ppermute | solution.py:43
  213.8 7.9 %select_reduce_fusion = bf16[16,128,128]{2,1,0:T(8,128)(2,1)S(1)} fusion(f32[16,16,128,128]{3,2,1,0:T(8,128)} %constant_dynamic-update-slice_fusion, pred[16]{0:T(512)(128)(4,1)S(1)} %iota_compare_fusion.3), kind=kLoop, calls=%fused_computation.3 | loop fusion | flops 8126464 | bytes 17301520 | tf_op jit(solution)/shard_map/reduce_sum | solution.py:54
  229.5 23.3 %scatter_custom_fusion = bf16[1536,2048]{1,0:T(8,128)(2,1)} fusion(s32[1024]{0:T(1024)S(1)} %bitcast.123, bf16[256,2048]{1,0:T(8,128)(2,1)} %fusion.26, s32[1024]{0:T(1024)S(1)} %broadcast_clamp_fusion.1, bf16[]{:T(256)} %constant.144.clone.1), kind=kCustom, calls=%fused_computation.20 | custom fusion | bytes 6291968 | tf_op jit(solution)/shard_map/scatter | solution.py:83
  252.8 82.9 %all_to_all.10 = bf16[8,192,2048]{2,1,0:T(8,128)(2,1)S(1)} all-to-all(bf16[8,192,2048]{2,1,0:T(8,128)(2,1)} %bitcast.110), channel_id=1, replica_groups=mesh['seq'=16,'exp'=8] {'exp'}, dimensions={0} | all-to-all | bytes 12582912 | tf_op jit(solution)/shard_map/all_to_all | solution.py:88
  335.7 2.6 copy-done.1
  338.3 13.4 %fusion.6 = f32[8,192,1408]{2,1,0:T(8,128)} fusion(bf16[8,192,2048]{2,1,0:T(8,128)(2,1)S(1)} %all_to_all.10, bf16[1,2048,1408]{2,1,0:T(8,128)(2,1)} %param.20), kind=kOutput, calls=%fused_computation.14 | convolution fusion | flops 8858370048 | bytes 20709376 | tf_op jit(solution)/shard_map/gend,edf->genf/dot_general | solution.py:92
  351.7 28.7 %fusion.9 = bf16[8,192,2048]{2,1,0:T(8,128)(2,1)} fusion(bf16[1,1408,2048]{2,1,0:T(8,128)(2,1)} %param.21, f32[8,192,1408]{2,1,0:T(8,128)} %fusion.6, bf16[8,192,2048]{2,1,0:T(8,128)(2,1)} %copy-done.1, bf16[1,2048,1408]{2,1,0:T(8,128)(2,1)} %param.19), kind=kOutput, calls=%fused_computation.17 | convolution fusion | flops 17732861952 | bytes 32768000 | tf_op jit(solution)/shard_map/genf,efd->gend/dot_general | solution.py:94
  380.4 6.0 %all-to-all-start.1 = ((bf16[8,192,2048]{2,1,0:T(8,128)(2,1)}), bf16[8,192,2048]{2,1,0:T(8,128)(2,1)}, u32[]{:S(2)}, u32[]{:S(2)}) async-start(bf16[8,192,2048]{2,1,0:T(8,128)(2,1)} %fusion.9), calls=%async_computation.1 | async-start | bytes 12582912 | tf_op jit(solution)/shard_map/all_to_all | solution.py:96
  388.4 69.2 %all-to-all-done.1 = bf16[8,192,2048]{2,1,0:T(8,128)(2,1)} async-done(((bf16[8,192,2048]{2,1,0:T(8,128)(2,1)}), bf16[8,192,2048]{2,1,0:T(8,128)(2,1)}, u32[]{:S(2)}, u32[]{:S(2)}) %all-to-all-start.1) | async-done | bytes 6291488 | tf_op jit(solution)/shard_map/all_to_all | solution.py:96
  457.6 12.4 %gather_fusion = bf16[1024,2048]{1,0:T(8,128)(2,1)} fusion(bf16[1536,2048]{1,0:T(8,128)(2,1)} %bitcast.26, s32[1024]{0:T(1024)S(1)} %broadcast_clamp_fusion), kind=kCustom, calls=%fused_computation.1 | custom fusion | bytes 8392704 | tf_op jit(solution)/shard_map/gather | solution.py:97
  470.0 8.3 %reshape.198 = f32[256,4,2048]{2,1,0:T(4,128)} reshape(bf16[1024,2048]{1,0:T(8,128)(2,1)} %gather_fusion) | data formatting | bytes 12582912 | tf_op jit(solution)/shard_map/convert_element_type | solution.py:98
  478.3 11.5 %multiply_reduce_fusion = f32[256,2048]{1,0:T(8,128)} fusion(f32[256,4,2048]{2,1,0:T(4,128)} %reshape.198, f32[256,4]{1,0:T(8,128)S(1)} %copy.41), kind=kLoop, calls=%fused_computation.11 | loop fusion | flops 3670016 | bytes 10489856 | tf_op jit(solution)/shard_map/reduce_sum | solution.py:98
  489.8 3.1 fusion.27
  (92 shorter events, 41.8 us)
Async XLA Ops:
  2.9 117.0 %copy-start.15 = (s32[1,256,4]{1,2,0:T(4,128)S(1)}, s32[1,256,4]{1,2,0:T(4,128)}, u32[]{:S(2)}) copy-start(s32[1,256,4]{1,2,0:T(4,128)} %param.17) | copy-start | bytes 12292
  12.3 29.6 %collective-permute-start = (f32[1,16,128,128]{3,2,1,0:T(8,128)S(1)}, f32[1,16,128,128]{3,2,1,0:T(8,128)S(1)}, u32[]{:S(2)}, u32[]{:S(2)}) collective-permute-start(f32[1,16,128,128]{3,2,1,0:T(8,128)S(1)} %get-tuple-element.8), channel_id=1, source_target_pairs={{0,8},{8,16},{16,24},{24,32},{32,40},{40,48},{48,56},{56,64},{64,7... | collective-permute-start | bytes 3145736 | tf_op jit(solution)/shard_map/ppermute | solution.py:43
  14.3 27.6 %collective-permute-start.1 = (f32[1,16,128,128]{3,2,1,0:T(8,128)S(1)}, f32[1,16,128,128]{3,2,1,0:T(8,128)S(1)}, u32[]{:S(2)}, u32[]{:S(2)}) collective-permute-start(f32[1,16,128,128]{3,2,1,0:T(8,128)S(1)} %get-tuple-element.8), channel_id=1, source_target_pairs={{0,120},{8,0},{16,8},{24,16},{32,24},{40,32},{48,40},{56,48},{64,5... | collective-permute-start | bytes 3145736 | tf_op jit(solution)/shard_map/ppermute | solution.py:48
  41.9 77.9 %copy-start.5 = (f32[1,16,128,128]{3,2,1,0:T(8,128)}, f32[1,16,128,128]{3,2,1,0:T(8,128)S(1)}, u32[]{:S(2)}) copy-start(f32[1,16,128,128]{3,2,1,0:T(8,128)S(1)} %collective-permute-done) | copy-start | bytes 3145732
  41.9 26.8 %collective-permute-start.2 = (f32[1,16,128,128]{3,2,1,0:T(8,128)S(1)}, f32[1,16,128,128]{3,2,1,0:T(8,128)S(1)}, u32[]{:S(2)}, u32[]{:S(2)}) collective-permute-start(f32[1,16,128,128]{3,2,1,0:T(8,128)S(1)} %collective-permute-done), channel_id=1, source_target_pairs={{0,8},{8,16},{16,24},{24,32},{32,40},{40,48},{48,56},{56,64},{64,7... | collective-permute-start | bytes 3145736 | tf_op jit(solution)/shard_map/ppermute | solution.py:43
  41.9 77.9 %copy-start.6 = (f32[1,16,128,128]{3,2,1,0:T(8,128)}, f32[1,16,128,128]{3,2,1,0:T(8,128)S(1)}, u32[]{:S(2)}) copy-start(f32[1,16,128,128]{3,2,1,0:T(8,128)S(1)} %collective-permute-done.1) | copy-start | bytes 3145732
  41.9 26.8 %collective-permute-start.3 = (f32[1,16,128,128]{3,2,1,0:T(8,128)S(1)}, f32[1,16,128,128]{3,2,1,0:T(8,128)S(1)}, u32[]{:S(2)}, u32[]{:S(2)}) collective-permute-start(f32[1,16,128,128]{3,2,1,0:T(8,128)S(1)} %collective-permute-done.1), channel_id=1, source_target_pairs={{0,120},{8,0},{16,8},{24,16},{32,24},{40,32},{48,40},{56,48},{64,5... | collective-permute-start | bytes 3145736 | tf_op jit(solution)/shard_map/ppermute | solution.py:48
  68.7 51.1 %copy-start.7 = (f32[1,16,128,128]{3,2,1,0:T(8,128)}, f32[1,16,128,128]{3,2,1,0:T(8,128)S(1)}, u32[]{:S(2)}) copy-start(f32[1,16,128,128]{3,2,1,0:T(8,128)S(1)} %collective-permute-done.2) | copy-start | bytes 3145732
  68.7 25.9 %collective-permute-start.4 = (f32[1,16,128,128]{3,2,1,0:T(8,128)S(1)}, f32[1,16,128,128]{3,2,1,0:T(8,128)S(1)}, u32[]{:S(2)}, u32[]{:S(2)}) collective-permute-start(f32[1,16,128,128]{3,2,1,0:T(8,128)S(1)} %collective-permute-done.2), channel_id=1, source_target_pairs={{0,8},{8,16},{16,24},{24,32},{32,40},{40,48},{48,56},{56,64},{64,7... | collective-permute-start | bytes 3145736 | tf_op jit(solution)/shard_map/ppermute | solution.py:43
  68.7 51.1 %copy-start.10 = (f32[1,16,128,128]{3,2,1,0:T(8,128)}, f32[1,16,128,128]{3,2,1,0:T(8,128)S(1)}, u32[]{:S(2)}) copy-start(f32[1,16,128,128]{3,2,1,0:T(8,128)S(1)} %collective-permute-done.3) | copy-start | bytes 3145732
  68.7 25.9 %collective-permute-start.5 = (f32[1,16,128,128]{3,2,1,0:T(8,128)S(1)}, f32[1,16,128,128]{3,2,1,0:T(8,128)S(1)}, u32[]{:S(2)}, u32[]{:S(2)}) collective-permute-start(f32[1,16,128,128]{3,2,1,0:T(8,128)S(1)} %collective-permute-done.3), channel_id=1, source_target_pairs={{0,120},{8,0},{16,8},{24,16},{32,24},{40,32},{48,40},{56,48},{64,5... | collective-permute-start | bytes 3145736 | tf_op jit(solution)/shard_map/ppermute | solution.py:48
  94.6 25.2 %copy-start.12 = (f32[1,16,128,128]{3,2,1,0:T(8,128)}, f32[1,16,128,128]{3,2,1,0:T(8,128)S(1)}, u32[]{:S(2)}) copy-start(f32[1,16,128,128]{3,2,1,0:T(8,128)S(1)} %collective-permute-done.4) | copy-start | bytes 3145732
  94.6 25.2 %collective-permute-start.6 = (f32[1,16,128,128]{3,2,1,0:T(8,128)S(1)}, f32[1,16,128,128]{3,2,1,0:T(8,128)}, u32[]{:S(2)}, u32[]{:S(2)}) collective-permute-start(f32[1,16,128,128]{3,2,1,0:T(8,128)S(1)} %collective-permute-done.4), channel_id=1, source_target_pairs={{0,8},{8,16},{16,24},{24,32},{32,40},{40,48},{48,56},{56,64},{64,7... | collective-permute-start | bytes 3145736 | tf_op jit(solution)/shard_map/ppermute | solution.py:43
  94.6 33.1 %copy-start.8 = (f32[1,16,128,128]{3,2,1,0:T(8,128)}, f32[1,16,128,128]{3,2,1,0:T(8,128)S(1)}, u32[]{:S(2)}) copy-start(f32[1,16,128,128]{3,2,1,0:T(8,128)S(1)} %collective-permute-done.5) | copy-start | bytes 3145732
  94.6 27.8 %collective-permute-start.7 = (f32[1,16,128,128]{3,2,1,0:T(8,128)S(1)}, f32[1,16,128,128]{3,2,1,0:T(8,128)}, u32[]{:S(2)}, u32[]{:S(2)}) collective-permute-start(f32[1,16,128,128]{3,2,1,0:T(8,128)S(1)} %collective-permute-done.5), channel_id=1, source_target_pairs={{0,120},{8,0},{16,8},{24,16},{32,24},{40,32},{48,40},{56,48},{64,5... | collective-permute-start | bytes 3145736 | tf_op jit(solution)/shard_map/ppermute | solution.py:48
  119.8 24.6 %collective-permute-start.8 = (f32[1,16,128,128]{3,2,1,0:T(8,128)}, f32[1,16,128,128]{3,2,1,0:T(8,128)}, u32[]{:S(2)}, u32[]{:S(2)}) collective-permute-start(f32[1,16,128,128]{3,2,1,0:T(8,128)} %collective-permute-done.6), channel_id=1, source_target_pairs={{0,8},{8,16},{16,24},{24,32},{32,40},{40,48},{48,56},{56,64},{64,7... | collective-permute-start | bytes 3145736 | tf_op jit(solution)/shard_map/ppermute | solution.py:43
  122.5 24.8 %collective-permute-start.9 = (f32[1,16,128,128]{3,2,1,0:T(8,128)}, f32[1,16,128,128]{3,2,1,0:T(8,128)}, u32[]{:S(2)}, u32[]{:S(2)}) collective-permute-start(f32[1,16,128,128]{3,2,1,0:T(8,128)} %collective-permute-done.7), channel_id=1, source_target_pairs={{0,120},{8,0},{16,8},{24,16},{32,24},{40,32},{48,40},{56,48},{64,5... | collective-permute-start | bytes 3145736 | tf_op jit(solution)/shard_map/ppermute | solution.py:48
  129.1 45.9 %copy-start.3 = (bf16[32,8,16,128]{3,2,1,0:T(8,128)(2,1)}, bf16[32,8,16,128]{3,2,1,0:T(8,128)(2,1)S(1)}, u32[]{:S(2)}) copy-start(bf16[32,8,16,128]{3,2,1,0:T(8,128)(2,1)S(1)} %copy.44) | copy-start | bytes 3145732
  144.4 23.7 %collective-permute-start.10 = (f32[1,16,128,128]{3,2,1,0:T(8,128)}, f32[1,16,128,128]{3,2,1,0:T(8,128)}, u32[]{:S(2)}, u32[]{:S(2)}) collective-permute-start(f32[1,16,128,128]{3,2,1,0:T(8,128)} %collective-permute-done.8), channel_id=1, source_target_pairs={{0,8},{8,16},{16,24},{24,32},{32,40},{40,48},{48,56},{56,64},{64,7... | collective-permute-start | bytes 3145736 | tf_op jit(solution)/shard_map/ppermute | solution.py:43
  147.2 27.8 %copy-start.11 = (f32[1,16,128,128]{3,2,1,0:T(8,128)S(1)}, f32[1,16,128,128]{3,2,1,0:T(8,128)}, u32[]{:S(2)}) copy-start(f32[1,16,128,128]{3,2,1,0:T(8,128)} %copy-done.10) | copy-start | bytes 3145732
  147.2 34.8 %copy-start.9 = (f32[1,16,128,128]{3,2,1,0:T(8,128)S(1)}, f32[1,16,128,128]{3,2,1,0:T(8,128)}, u32[]{:S(2)}) copy-start(f32[1,16,128,128]{3,2,1,0:T(8,128)} %copy-done.8) | copy-start | bytes 3145732
  147.2 30.0 %collective-permute-start.11 = (f32[1,16,128,128]{3,2,1,0:T(8,128)}, f32[1,16,128,128]{3,2,1,0:T(8,128)}, u32[]{:S(2)}, u32[]{:S(2)}) collective-permute-start(f32[1,16,128,128]{3,2,1,0:T(8,128)} %collective-permute-done.9), channel_id=1, source_target_pairs={{0,120},{8,0},{16,8},{24,16},{32,24},{40,32},{48,40},{56,48},{64,5... | collective-permute-start | bytes 3145736 | tf_op jit(solution)/shard_map/ppermute | solution.py:48
  152.3 23.8 %copy-start.13 = (f32[1,16,128,128]{3,2,1,0:T(8,128)S(1)}, f32[1,16,128,128]{3,2,1,0:T(8,128)}, u32[]{:S(2)}) copy-start(f32[1,16,128,128]{3,2,1,0:T(8,128)} %copy-done.12) | copy-start | bytes 3145732
  168.1 22.7 %collective-permute-start.12 = (f32[1,16,128,128]{3,2,1,0:T(8,128)}, f32[1,16,128,128]{3,2,1,0:T(8,128)S(1)}, u32[]{:S(2)}, u32[]{:S(2)}) collective-permute-start(f32[1,16,128,128]{3,2,1,0:T(8,128)} %collective-permute-done.10), channel_id=1, source_target_pairs={{0,8},{8,16},{16,24},{24,32},{32,40},{40,48},{48,56},{56,64},{64,7... | collective-permute-start | bytes 3145736 | tf_op jit(solution)/shard_map/ppermute | solution.py:43
  177.2 28.8 %collective-permute-start.13 = (f32[1,16,128,128]{3,2,1,0:T(8,128)}, f32[1,16,128,128]{3,2,1,0:T(8,128)S(1)}, u32[]{:S(2)}, u32[]{:S(2)}) collective-permute-start(f32[1,16,128,128]{3,2,1,0:T(8,128)} %collective-permute-done.11), channel_id=1, source_target_pairs={{0,120},{8,0},{16,8},{24,16},{32,24},{40,32},{48,40},{56,48},{64,5... | collective-permute-start | bytes 3145736 | tf_op jit(solution)/shard_map/ppermute | solution.py:48
  190.8 21.8 %collective-permute-start.14 = (f32[1,16,128,128]{3,2,1,0:T(8,128)S(1)}, f32[1,16,128,128]{3,2,1,0:T(8,128)S(1)}, u32[]{:S(2)}, u32[]{:S(2)}) collective-permute-start(f32[1,16,128,128]{3,2,1,0:T(8,128)S(1)} %collective-permute-done.12), channel_id=1, source_target_pairs={{0,8},{8,16},{16,24},{24,32},{32,40},{40,48},{48,56},{56,64},{64,7... | collective-permute-start | bytes 3145736 | tf_op jit(solution)/shard_map/ppermute | solution.py:43
  213.8 8.0 %copy-start.4 = (bf16[32,8,16,128]{3,2,1,0:T(8,128)(2,1)S(1)}, bf16[32,8,16,128]{3,2,1,0:T(8,128)(2,1)}, u32[]{:S(2)}) copy-start(bf16[32,8,16,128]{3,2,1,0:T(8,128)(2,1)} %copy-done.3) | copy-start | bytes 3145732
  221.7 4.4 copy-start.2
  221.8 4.4 copy-start.14
  380.4 6.0 %copy-start.17 = (f32[1,256,4]{1,2,0:T(4,128)S(1)}, f32[1,256,4]{1,2,0:T(4,128)}, u32[]{:S(2)}) copy-start(f32[1,256,4]{1,2,0:T(4,128)} %param.18) | copy-start | bytes 12292
  380.4 77.2 %all-to-all-start.1 = ((bf16[8,192,2048]{2,1,0:T(8,128)(2,1)}), bf16[8,192,2048]{2,1,0:T(8,128)(2,1)}, u32[]{:S(2)}, u32[]{:S(2)}) async-start(bf16[8,192,2048]{2,1,0:T(8,128)(2,1)} %fusion.9), calls=%async_computation.1 | async-start | bytes 12582912 | tf_op jit(solution)/shard_map/all_to_all | solution.py:96
  478.3 11.5 %copy-start = (f32[1,256,2048]{2,1,0:T(8,128)S(1)}, f32[1,256,2048]{2,1,0:T(8,128)}, u32[]{:S(2)}) copy-start(f32[1,256,2048]{2,1,0:T(8,128)} %copy.36) | copy-start | bytes 6291460
  (2 other events, 6.8 us)
